TPU v7x, 32 devices: a whole 2x2x4 slice. The times are simulated.
32 devices in a mesh: tensor: 4 (over x, core), replica: 4 (over z), fsdp: 2 (over y).
Axes of the slice: x: 2, y: 2, z: 4, core: 2. Of those that a mesh axis runs over, the one named last changes fastest.
Arguments:
- gradients: bfloat16 [4, 128, 28672], P('replica', 'fsdp', 'tensor'), may hold values from -6 to 6
- seeds: int32 [2], replicated, may hold values from 0 to 1073741823
- adam_step: int32 [1], replicated, may hold values from 1 to 8
- first_moment: float32 [128, 28672], P(('fsdp', 'replica'), 'tensor'), may hold values from -0.6 to 0.6
- second_moment: float32 [128, 28672], P(('fsdp', 'replica'), 'tensor'), may hold values from 0.001 to 0.1
Outputs:
- new_first: float32 [128, 28672], P(('fsdp', 'replica'), 'tensor')
- new_second: float32 [128, 28672], P(('fsdp', 'replica'), 'tensor')
- step_update: float32 [128, 28672], P(('fsdp', 'replica'), 'tensor')
All inputs are finite; a program needn't handle non-finite values.
Results may differ from a plain program's by a relative error of at most 0.012.
The roundings to bfloat16 on the way count: a program that leaves them out, or rounds other values in their place, can miss the bound.
Values may be sent and summed in bfloat16 or wider, within the bound.
No kernel may reach another device: no remote copies, remote signals or barrier semaphores. Data moves between devices by JAX's collectives and lax.ppermute only.
A program may use at most 64 MiB of HBM per device.

v0:
```python
import math
import jax
import jax.numpy as jnp
from jax import lax
from jax.sharding import PartitionSpec as P

RANK = 512
GROUP = ("fsdp", "replica")


def scramble(value):
    value = value ^ lax.shift_right_logical(value, jnp.full_like(value, 16))
    value = value * jnp.int32(-2048144789)
    value = value ^ lax.shift_right_logical(value, jnp.full_like(value, 13))
    value = value * jnp.int32(-1028477387)
    value = value ^ lax.shift_right_logical(value, jnp.full_like(value, 16))
    return value


def projection_block(first_column, columns, rank, seeds):
    seed_key = seeds[0] ^ seeds[1] * jnp.int32(668265263)
    column = lax.broadcasted_iota(jnp.int32, (columns, rank), 0) + first_column
    entry = lax.broadcasted_iota(jnp.int32, (columns, rank), 1)
    counter = (column * jnp.int32(rank) + entry) * jnp.int32(2)
    hash_a = scramble(counter * jnp.int32(-1640531535) ^ seed_key)
    hash_b = scramble((counter + jnp.int32(1)) * jnp.int32(-1640531535) ^ seed_key)
    inverse = 1.0 / 16777216.0
    uniform_a = (
        lax.shift_right_logical(hash_a, jnp.full_like(hash_a, 8)).astype(jnp.float32) + 0.5
    ) * inverse
    uniform_b = (
        lax.shift_right_logical(hash_b, jnp.full_like(hash_b, 8)).astype(jnp.float32) + 0.5
    ) * inverse
    gauss = jnp.sqrt(-2.0 * jnp.log(uniform_a)) * jnp.cos(6.283185307179586 * uniform_b)
    return (gauss * rank ** (-0.5)).astype(jnp.bfloat16)


def adam(first_moment, second_moment, estimate, adam_step):
    new_first = 0.9 * first_moment + 0.1 * estimate
    new_second = 0.95 * second_moment + 0.05 * estimate * estimate
    step_float = adam_step[0].astype(jnp.float32)
    fix_first = 1.0 - jnp.power(jnp.float32(0.9), step_float)
    fix_second = 1.0 - jnp.power(jnp.float32(0.95), step_float)
    step_update = new_first / fix_first / (jnp.sqrt(new_second / fix_second) + 1e-08)
    return (new_first, new_second, step_update)


def per_device_whole(gradients, seeds, adam_step, first_moment, second_moment):
    gradient = gradients[0]
    columns = gradient.shape[1]
    replicas = lax.axis_size("replica")
    column_start = lax.axis_index("tensor") * jnp.int32(columns)
    piece_cols = math.gcd(columns, 512)
    blocks = columns // piece_cols
    starts = column_start + lax.iota(jnp.int32, blocks) * jnp.int32(piece_cols)
    tiles = lax.map(lambda first: projection_block(first, piece_cols, RANK, seeds), starts)
    projection = tiles.reshape(columns, RANK)
    partial_value = jnp.dot(gradient, projection, preferred_element_type=jnp.float32) * (
        1.0 / replicas
    )
    share = lax.psum_scatter(partial_value, "replica", scatter_dimension=0, tiled=True)
    sketch = lax.psum(share, "tensor")
    sketch_rounded = sketch.astype(jnp.bfloat16)
    estimate = lax.dot_general(
        sketch_rounded, projection, (((1,), (1,)), ((), ())), preferred_element_type=jnp.float32
    )
    return adam(first_moment, second_moment, estimate, adam_step)


def per_device(gradients, seeds, adam_step, first_moment, second_moment):
    gradient = gradients[0]
    rows, columns = gradient.shape
    n_fsdp = lax.axis_size("fsdp")
    n_rep = lax.axis_size("replica")
    n_group = n_fsdp * n_rep
    width = columns // n_group
    if columns % (n_group * 128) != 0:
        return per_device_whole(gradients, seeds, adam_step, first_moment, second_moment)
    member = lax.axis_index(GROUP)
    first = lax.axis_index("tensor") * jnp.int32(columns) + member * jnp.int32(width)
    projection = lax.optimization_barrier(projection_block(first, width, RANK, seeds))
    pieces = gradient.reshape(rows, n_group, width).transpose(1, 0, 2)
    held = lax.all_to_all(pieces, GROUP, 0, 0, tiled=True)
    held = held.reshape(n_fsdp, n_rep, rows, width)
    partial_value = None
    for r in range(n_rep):
        term = lax.dot_general(
            held[:, r], projection, (((2,), (0,)), ((), ())), preferred_element_type=jnp.float32
        )
        partial_value = term if partial_value is None else partial_value + term
    partial_value = partial_value.reshape(n_fsdp * rows, RANK) * (1.0 / n_rep)
    sketch = lax.psum(partial_value, ("tensor",) + GROUP)
    sketch_rounded = sketch.astype(jnp.bfloat16)
    estimate = lax.dot_general(
        sketch_rounded, projection, (((1,), (1,)), ((), ())), preferred_element_type=jnp.float32
    )
    out_rows = first_moment.shape[0]
    estimate = estimate.reshape(n_group, out_rows, width)
    estimate = lax.all_to_all(estimate, GROUP, 0, 0, tiled=True)
    estimate = estimate.transpose(1, 0, 2).reshape(out_rows, columns)
    return adam(first_moment, second_moment, estimate, adam_step)


def solution(mesh):
    placed = (
        P("replica", "fsdp", "tensor"),
        P(),
        P(),
        P(("fsdp", "replica"), "tensor"),
        P(("fsdp", "replica"), "tensor"),
    )
    return jax.shard_map(
        per_device,
        mesh=mesh,
        in_specs=placed,
        out_specs=(
            P(("fsdp", "replica"), "tensor"),
            P(("fsdp", "replica"), "tensor"),
            P(("fsdp", "replica"), "tensor"),
        ),
        check_vma=False,
    )
```

profile of v0, /device:TPU:0, one launch (start us, length us, event | category | flops | bytes accessed | tf_op | source)
XLA Modules:
  0.0 96.1 jit_solution(1003083572574440337)
XLA Ops:
  0.6 1.3 %copy.31 = bf16[8,8,8,896]{3,2,1,0:T(8,128)(2,1)S(1)} copy(bf16[8,8,8,896]{3,1,2,0:T(8,128)(2,1)} %bitcast.55) | data formatting | bytes 1835008
  2.0 1.1 %copy.20 = bf16[8,64,896]{2,1,0:T(8,128)(2,1)} copy(bf16[8,64,896]{2,0,1:T(8,128)(2,1)S(1)} %bitcast.51) | data formatting | bytes 1835008 | tf_op jit(solution)/shard_map/transpose | solution.py:82
  3.1 0.0 copy-start.2
  3.1 7.4 %all-to-all-start = ((bf16[8,64,896]{2,1,0:T(8,128)(2,1)}), bf16[8,64,896]{2,1,0:T(8,128)(2,1)S(1)}, u32[]{:S(2)}, u32[]{:S(2)}) async-start(bf16[8,64,896]{2,1,0:T(8,128)(2,1)} %copy.20), calls=%async_computation | async-start | bytes 1835008 | tf_op jit(solution)/shard_map/all_to_all | solution.py:83
  10.5 0.0 copy-done.2
  10.5 0.6 fusion.29
  12.4 9.2 %fusion.18 = bf16[896,512]{1,0:T(8,128)(2,1)S(1)} fusion(s32[]{:T(128)} %bitcast, s32[896]{0:T(1024)S(1)} %add_multiply_fusion), kind=kLoop, calls=%fused_computation.24 | loop fusion | flops 16056320 | bytes 921092 | tf_op jit(solution)/shard_map/convert_element_type | solution.py:35
  21.6 12.7 %all-to-all-done = bf16[8,64,896]{2,1,0:T(8,128)(2,1)S(1)} async-done(((bf16[8,64,896]{2,1,0:T(8,128)(2,1)}), bf16[8,64,896]{2,1,0:T(8,128)(2,1)S(1)}, u32[]{:S(2)}, u32[]{:S(2)}) %all-to-all-start) | async-done | bytes 917536 | tf_op jit(solution)/shard_map/all_to_all | solution.py:83
  34.3 0.3 fusion.23
  34.6 0.3 convolution_add_fusion.2
  34.9 0.3 convolution_add_fusion.1
  35.3 0.3 fusion.19
  35.6 40.4 %all-reduce.1 = bf16[128,512]{1,0:T(8,128)(2,1)S(1)} all-reduce(f32[128,512]{1,0:T(8,128)S(1)} %bitcast.54), channel_id=1, replica_groups=mesh['tensor'=4,'replica'=4,'fsdp'=2] {'tensor','fsdp','replica'}, use_global_device_ids=true, to_apply=%region_0.0 | all-reduce | flops 65536 | bytes 393216 | tf_op jit(solution)/shard_map/psum | solution.py:92
  76.0 1.2 %fusion.30 = f32[128,896]{1,0:T(8,128)} fusion(bf16[128,512]{1,0:T(8,128)(2,1)S(1)} %all-reduce.1, bf16[896,512]{1,0:T(8,128)(2,1)S(1)} %fusion.18), kind=kOutput, calls=%fused_computation.46 | convolution fusion | flops 117440512 | bytes 1507328 | tf_op jit(solution)/shard_map/dot_general | solution.py:94
  77.3 0.0 copy-start
  77.3 0.0 copy-start.1
  77.3 4.4 %all-to-all-start.1 = ((f32[8,16,896]{2,1,0:T(8,128)}), f32[8,16,896]{2,1,0:T(8,128)S(1)}, u32[]{:S(2)}, u32[]{:S(2)}) async-start(f32[8,16,896]{2,1,0:T(8,128)} %bitcast.10), calls=%async_computation.1 | async-start | bytes 917504 | tf_op jit(solution)/shard_map/all_to_all | solution.py:99
  82.3 12.4 %all-to-all-done.1 = f32[8,16,896]{2,1,0:T(8,128)S(1)} async-done(((f32[8,16,896]{2,1,0:T(8,128)}), f32[8,16,896]{2,1,0:T(8,128)S(1)}, u32[]{:S(2)}, u32[]{:S(2)}) %all-to-all-start.1) | async-done | bytes 458784 | tf_op jit(solution)/shard_map/all_to_all | solution.py:99
  94.8 0.0 copy-done
  94.8 0.0 copy-done.1
  94.8 1.2 %multiply_divide_fusion = (f32[16,7168]{1,0:T(8,128)}, f32[16,7168]{1,0:T(8,128)}, f32[16,7168]{1,0:T(8,128)}) fusion(f32[]{:T(128)} %bitcast.13, f32[]{:T(128)} %bitcast.12, f32[16,7168]{1,0:T(8,128)S(1)} %bitcast.52, f32[16,7168]{1,0:T(8,128)S(1)} %copy-done, f32[16,7168]{1,0:T(8,128)S(1)} %copy-done.1), kind=kLoop, calls=%fused_computation.36 | loop fusion | flops 1261568 | bytes 2752520 | tf_op jit(solution)/shard_map/div | solution.py:44
  (2 shorter events, 0.0 us)
Async XLA Ops:
  3.1 7.4 %copy-start.2 = (s32[2]{0:T(128)S(1)}, s32[2]{0:T(128)}, u32[]{:S(2)}) copy-start(s32[2]{0:T(128)} %param.6) | copy-start | bytes 28
  3.1 31.3 %all-to-all-start = ((bf16[8,64,896]{2,1,0:T(8,128)(2,1)}), bf16[8,64,896]{2,1,0:T(8,128)(2,1)S(1)}, u32[]{:S(2)}, u32[]{:S(2)}) async-start(bf16[8,64,896]{2,1,0:T(8,128)(2,1)} %copy.20), calls=%async_computation | async-start | bytes 1835008 | tf_op jit(solution)/shard_map/all_to_all | solution.py:83
  77.3 17.6 %copy-start = (f32[16,7168]{1,0:T(8,128)S(1)}, f32[16,7168]{1,0:T(8,128)}, u32[]{:S(2)}) copy-start(f32[16,7168]{1,0:T(8,128)} %param.9) | copy-start | bytes 1376260
  77.3 17.6 %copy-start.1 = (f32[16,7168]{1,0:T(8,128)S(1)}, f32[16,7168]{1,0:T(8,128)}, u32[]{:S(2)}) copy-start(f32[16,7168]{1,0:T(8,128)} %param.8) | copy-start | bytes 1376260
  77.3 17.5 %all-to-all-start.1 = ((f32[8,16,896]{2,1,0:T(8,128)}), f32[8,16,896]{2,1,0:T(8,128)S(1)}, u32[]{:S(2)}, u32[]{:S(2)}) async-start(f32[8,16,896]{2,1,0:T(8,128)} %bitcast.10), calls=%async_computation.1 | async-start | bytes 917504 | tf_op jit(solution)/shard_map/all_to_all | solution.py:99
where the time goes:
time: 96.5 us; the launch traced here: 96.1 us
  blocking collectives  40.4 us (42%)
  waiting for transfers between devices  25.1 us (26%)
  starting transfers between devices  11.8 us (12%)
  other arithmetic  10.4 us (11%)
  local copies, waits for them, and re-layouts  3.04 us (3%)
  between operations  2.75 us (3%)
  matrix products  2.47 us (3%)
    psum x1, blocking collectives, per_device(): sketch = lax.psum(partial_value, ('tensor',) + GROUP)  40.4 us
    all_to_all x1, waiting for transfers between devices, per_device(): held = lax.all_to_all(pieces, GROUP, 0, 0, tiled=True)  12.7 us
    all_to_all x1, waiting for transfers between devices, per_device(): estimate = lax.all_to_all(estimate, GROUP, 0, 0, tiled=True)  12.4 us
    convert_element_type x1, other arithmetic, projection_block(): return (gauss * rank ** (-0.5)).astype(jnp.bfloat16)  9.2 us
    all_to_all x1, starting transfers between devices, per_device(): held = lax.all_to_all(pieces, GROUP, 0, 0, tiled=True)  7.44 us
    all_to_all x1, starting transfers between devices, per_device(): estimate = lax.all_to_all(estimate, GROUP, 0, 0, tiled=True)  4.35 us
  transfers between devices with their start and end apart: 2, of which 2 were waited for; matrix products, arithmetic and copies ran while one was open for 10% of the time, Pallas kernels for 0%

commit v1 on v0

--- a/solution.py
+++ b/solution.py
@@ -89,7 +89,7 @@
         )
         partial_value = term if partial_value is None else partial_value + term
     partial_value = partial_value.reshape(n_fsdp * rows, RANK) * (1.0 / n_rep)
-    sketch = lax.psum(partial_value, ("tensor",) + GROUP)
+    sketch = jnp.sum(lax.all_gather(partial_value, ("tensor",) + GROUP), axis=0)
     sketch_rounded = sketch.astype(jnp.bfloat16)
     estimate = lax.dot_general(
         sketch_rounded, projection, (((1,), (1,)), ((), ())), preferred_element_type=jnp.float32

time: 96.5 us -> 150 us (1.55)
  waiting for transfers between devices: 25.1 us -> 101 us
  blocking collectives: 40.4 us -> 0 us
  between operations: 2.75 us -> 16.2 us
  other arithmetic: 10.4 us -> 14.7 us
    all_gather x0 -> x1, waiting for transfers between devices: none -> 74.5 us  [per_device(): sketch = jnp.sum(lax.all_gather(partial_value, ('tensor',) + GROUP), axis=0)]
    psum x1 -> x0, blocking collectives: 40.4 us -> none  [per_device(): sketch = lax.psum(partial_value, ('tensor',) + GROUP)]
    reduce_sum x0 -> x1, other arithmetic: none -> 4.26 us  [per_device(): sketch = jnp.sum(lax.all_gather(partial_value, ('tensor',) + GROUP), axis=0)]
  transfers between devices with their start and end apart: 2 -> 3, of which waited for: 2 -> 3; matrix products, arithmetic and copies ran while one was open for 10% -> 7% of each run, Pallas kernels for 0% -> 0%
where the time goes in v1:
time: 150 us; the launch traced here: 149 us
  waiting for transfers between devices  101 us (67%)
  between operations  16.2 us (11%)
  other arithmetic  14.7 us (10%)
  starting transfers between devices  11.5 us (8%)
  matrix products  3.18 us (2%)
  local copies, waits for them, and re-layouts  3.03 us (2%)
    all_gather x1, waiting for transfers between devices, per_device(): sketch = jnp.sum(lax.all_gather(partial_value, ('tensor',) + GROUP), axis=0)  74.5 us
    all_to_all x1, waiting for transfers between devices, per_device(): estimate = lax.all_to_all(estimate, GROUP, 0, 0, tiled=True)  13.7 us
    all_to_all x1, waiting for transfers between devices, per_device(): held = lax.all_to_all(pieces, GROUP, 0, 0, tiled=True)  12.6 us
    convert_element_type x1, other arithmetic, projection_block(): return (gauss * rank ** (-0.5)).astype(jnp.bfloat16)  9.2 us
    all_to_all x1, starting transfers between devices, per_device(): held = lax.all_to_all(pieces, GROUP, 0, 0, tiled=True)  7.31 us
    reduce_sum x1, other arithmetic, per_device(): sketch = jnp.sum(lax.all_gather(partial_value, ('tensor',) + GROUP), axis=0)  4.26 us
    all_to_all x1, starting transfers between devices, per_device(): estimate = lax.all_to_all(estimate, GROUP, 0, 0, tiled=True)  4.13 us
  transfers between devices with their start and end apart: 3, of which 3 were waited for; matrix products, arithmetic and copies ran while one was open for 7% of the time, Pallas kernels for 0%

profile of v1, /device:TPU:0, one launch (start us, length us, event | category | flops | bytes accessed | tf_op | source)
XLA Modules:
  0.0 149.4 jit_solution(626135453077514456)
XLA Ops:
  7.2 1.3 copy.31
  8.5 0.0 copy-start.2
  8.5 1.1 copy.20
  9.6 7.3 %all-to-all-start = ((bf16[8,64,896]{2,1,0:T(8,128)(2,1)}), bf16[8,64,896]{2,1,0:T(8,128)(2,1)S(1)}, u32[]{:S(2)}, u32[]{:S(2)}) async-start(bf16[8,64,896]{2,1,0:T(8,128)(2,1)} %copy.20), calls=%async_computation | async-start | bytes 1835008 | tf_op jit(solution)/shard_map/all_to_all | solution.py:83
  16.9 0.0 all-gather.2.cloned.1.call-start
  16.9 0.0 copy-done.2
  17.0 0.6 fusion.29
  18.9 9.2 %fusion.18 = bf16[896,512]{1,0:T(8,128)(2,1)S(1)} fusion(s32[]{:T(128)} %bitcast, s32[896]{0:T(1024)S(1)} %add_multiply_fusion), kind=kLoop, calls=%fused_computation.24 | loop fusion | flops 16056320 | bytes 921092 | tf_op jit(solution)/shard_map/convert_element_type | solution.py:35
  28.1 12.6 %all-to-all-done = bf16[8,64,896]{2,1,0:T(8,128)(2,1)S(1)} async-done(((bf16[8,64,896]{2,1,0:T(8,128)(2,1)}), bf16[8,64,896]{2,1,0:T(8,128)(2,1)S(1)}, u32[]{:S(2)}, u32[]{:S(2)}) %all-to-all-start) | async-done | bytes 917536 | tf_op jit(solution)/shard_map/all_to_all | solution.py:83
  40.7 0.3 fusion.23
  41.0 0.3 convolution_add_fusion.2
  41.3 0.3 convolution_add_fusion.1
  41.7 1.0 fusion.19
  42.7 0.0 all-gather.2.cloned.1.call-update
  42.7 74.5 %all-gather.2.cloned.1.call-done = f32[32,128,512]{2,1,0:T(8,128)} async-done(((f32[1,128,512]{2,1,0:T(8,128)}), f32[32,128,512]{2,1,0:T(8,128)}) %all-gather.2.cloned.1.call-update) | async-done | bytes 8388624 | tf_op jit(solution)/shard_map/all_gather | solution.py:92
  117.2 4.3 %reduce_sum.9 = bf16[128,512]{1,0:T(8,128)(2,1)S(1)} reduce(f32[32,128,512]{2,1,0:T(8,128)} %all-gather.2.cloned.1.call-done, f32[]{:T(128)} %constant.67.clone.1), dimensions={0}, to_apply=%region_0.0 | reduce | flops 2031616 | bytes 8519684 | tf_op jit(solution)/shard_map/reduce_sum | solution.py:92
  121.5 0.0 copy-start
  121.5 0.0 copy-start.1
  121.5 1.2 fusion.30
  122.8 4.1 %all-to-all-start.1 = ((f32[8,16,896]{2,1,0:T(8,128)}), f32[8,16,896]{2,1,0:T(8,128)S(1)}, u32[]{:S(2)}, u32[]{:S(2)}) async-start(f32[8,16,896]{2,1,0:T(8,128)} %bitcast.10), calls=%async_computation.1 | async-start | bytes 917504 | tf_op jit(solution)/shard_map/all_to_all | solution.py:99
  127.6 13.7 %all-to-all-done.1 = f32[8,16,896]{2,1,0:T(8,128)S(1)} async-done(((f32[8,16,896]{2,1,0:T(8,128)}), f32[8,16,896]{2,1,0:T(8,128)S(1)}, u32[]{:S(2)}, u32[]{:S(2)}) %all-to-all-start.1) | async-done | bytes 458784 | tf_op jit(solution)/shard_map/all_to_all | solution.py:99
  141.3 0.0 copy-done
  141.3 0.0 copy-done.1
  141.3 1.2 multiply_divide_fusion
  (2 shorter events, 0.0 us)
Async XLA Ops:
  8.5 8.5 %copy-start.2 = (s32[2]{0:T(128)S(1)}, s32[2]{0:T(128)}, u32[]{:S(2)}) copy-start(s32[2]{0:T(128)} %param.6) | copy-start | bytes 28
  9.6 31.1 %all-to-all-start = ((bf16[8,64,896]{2,1,0:T(8,128)(2,1)}), bf16[8,64,896]{2,1,0:T(8,128)(2,1)S(1)}, u32[]{:S(2)}, u32[]{:S(2)}) async-start(bf16[8,64,896]{2,1,0:T(8,128)(2,1)} %copy.20), calls=%async_computation | async-start | bytes 1835008 | tf_op jit(solution)/shard_map/all_to_all | solution.py:83
  16.9 100.3 %all-gather.2.cloned.1.call-start = ((), (), s32[]{:S(2)}) async-start(), calls=%async_computation.2 | async-start | bytes 8650752 | tf_op jit(solution)/shard_map/all_gather | solution.py:92
  121.5 19.8 %copy-start = (f32[16,7168]{1,0:T(8,128)S(1)}, f32[16,7168]{1,0:T(8,128)}, u32[]{:S(2)}) copy-start(f32[16,7168]{1,0:T(8,128)} %param.9) | copy-start | bytes 1376260
  121.5 19.8 %copy-start.1 = (f32[16,7168]{1,0:T(8,128)S(1)}, f32[16,7168]{1,0:T(8,128)}, u32[]{:S(2)}) copy-start(f32[16,7168]{1,0:T(8,128)} %param.8) | copy-start | bytes 1376260
  122.8 18.5 %all-to-all-start.1 = ((f32[8,16,896]{2,1,0:T(8,128)}), f32[8,16,896]{2,1,0:T(8,128)S(1)}, u32[]{:S(2)}, u32[]{:S(2)}) async-start(f32[8,16,896]{2,1,0:T(8,128)} %bitcast.10), calls=%async_computation.1 | async-start | bytes 917504 | tf_op jit(solution)/shard_map/all_to_all | solution.py:99
Sparse Core Ops, SparseCore 0:
  42.8 74.3 all-gather.1
